TPU v7x, 256 devices: a whole 4x4x8 slice. The times are simulated.
256 devices in a mesh: pair: 128 (over x, z, y), aux: 2 (over core).
Axes of the slice: x: 4, y: 4, z: 8, core: 2. Of those that a mesh axis runs over, the one named last changes fastest.
Arguments:
- amplitudes: bfloat16 [16384, 128, 128], P('pair', 'aux'), may hold values from -6 to 6
- k_term: bfloat16 [16384, 128, 128], P('pair', 'aux'), may hold values from -6 to 6
- margin_table: bfloat16 [1024, 128, 128], P('pair'), may hold values from -0.5 to 0.5
- margin_index: int32 [16384], P('pair'), may hold values from 0 to 7
- factors: bfloat16 [128, 512, 128], P('pair', 'aux'), may hold values from -6 to 6
- vir_energy: float32 [16384, 128], P('pair'), may hold values from 0.5 to 3
- occ_energy: float32 [128], replicated, may hold values from -2 to -0.3
- pair_owner: int32 [16384, 1], P('pair'), may hold values from 0 to 127; in each aligned block of 128 rows (0 to 127, 128 to 255, ...) at most 2 rows name the same one
Outputs:
- updated: bfloat16 [16384, 128, 128], P('pair', 'aux')
Inputs may be any that keep to these rules, and one draw needn't show every extreme that they name: `pair_owner`: no more than 2 of the 128 pairs of one aligned block name the same owner. `margin_index`: an index into the 8 margin blocks that belong to the pair's aligned block of 128 pairs.
All inputs are finite; a program needn't handle non-finite values.
Results may differ from a plain program's by a relative error of at most 0.0055.
Values may be sent and summed in bfloat16 or wider, within the bound.
No kernel may reach another device: no remote copies, remote signals or barrier semaphores. Data moves between devices by JAX's collectives and lax.ppermute only.
A program may use at most 128 MiB of HBM per device.

v0:
```python
import jax
import jax.numpy as jnp
from jax import lax
from jax.sharding import PartitionSpec as P


def local(
    amplitudes, k_term, margin_table, margin_index, factors, vir_energy, occ_energy, pair_owner
):
    axis_pairs = lax.axis_size("pair")
    aux_count = lax.axis_size("aux")
    own_index = lax.axis_index("pair")
    aux_index = lax.axis_index("aux")
    pair_count = amplitudes.shape[0]
    row_count = amplitudes.shape[1]
    vir_width = amplitudes.shape[2]
    aux_rows = factors.shape[1]
    ovl_count = margin_table.shape[0]
    capacity = max(2, (2 * pair_count + axis_pairs - 1) // axis_pairs)
    cycle_scale = float(vir_width * aux_rows * aux_count * pair_count) ** (-0.5)
    own_factors = factors[0]
    full_amp = lax.all_gather(amplitudes, "aux", axis=1, tiled=True)
    block_pick = (margin_index[:, None] == jnp.arange(ovl_count, dtype=jnp.int32)[None, :]).astype(
        jnp.bfloat16
    )
    margin = jnp.einsum(
        "po,oab->pab", block_pick, margin_table, preferred_element_type=jnp.float32
    ).astype(jnp.bfloat16)
    halfway = jnp.einsum(
        "pca,pab->pcb", full_amp, margin, preferred_element_type=jnp.float32
    ).astype(jnp.bfloat16)
    rotated = jnp.einsum(
        "pac,pab->pcb", margin, halfway, preferred_element_type=jnp.float32
    ).astype(jnp.bfloat16)
    partial_value = jnp.einsum(
        "pca,qa->pcq", rotated, own_factors, preferred_element_type=jnp.float32
    ).astype(jnp.bfloat16)
    pair_dest = pair_owner[:, 0]
    owner_hits = (pair_dest[:, None] == jnp.arange(axis_pairs, dtype=jnp.int32)[None, :]).astype(
        jnp.int32
    )
    slot_rank = jnp.sum(jnp.cumsum(owner_hits, axis=0) * owner_hits, axis=1) - 1
    slot_index = pair_dest * capacity + slot_rank
    outgoing = (
        jnp.zeros((axis_pairs * capacity, vir_width, aux_rows), jnp.bfloat16)
        .at[slot_index]
        .set(partial_value)
    )
    outgoing = outgoing.reshape(axis_pairs, capacity, vir_width, aux_rows)
    incoming = lax.all_to_all(outgoing, "pair", split_axis=0, concat_axis=0, tiled=True)
    slot_ones = jnp.ones((axis_pairs, capacity), jnp.bfloat16)
    summed = jnp.einsum(
        "sk,skcq->cq", slot_ones, incoming, preferred_element_type=jnp.float32
    ).astype(jnp.bfloat16)
    local_cycle = jnp.dot(summed, own_factors, preferred_element_type=jnp.float32)
    cycle_sum = lax.psum(local_cycle, "aux")
    cycle_vals = (cycle_scale * cycle_sum).astype(jnp.bfloat16)
    cycle_rows = cycle_vals.shape[0]
    slot_back = jnp.broadcast_to(
        cycle_vals[None, None], (axis_pairs, capacity, cycle_rows, vir_width)
    )
    returned = lax.all_to_all(slot_back, "pair", split_axis=0, concat_axis=0, tiled=True)
    own_cycle = returned.reshape(axis_pairs * capacity, cycle_rows, vir_width)[slot_index]
    own_cycle = lax.dynamic_slice_in_dim(own_cycle, aux_index * row_count, row_count, 1)
    cycle_term = jnp.einsum("pca,pba->pcb", own_cycle, margin, preferred_element_type=jnp.float32)
    occ_total = occ_energy.shape[0]
    occ_first = jnp.zeros((pair_count,), jnp.int32) + own_index
    both_ids = jnp.concatenate([occ_first, pair_dest])
    occ_select = (both_ids[:, None] == jnp.arange(occ_total, dtype=jnp.int32)[None, :]).astype(
        jnp.float32
    )
    occ_values = jnp.sum(occ_select * occ_energy[None, :], axis=1)
    occ_sum = occ_values[:pair_count] + occ_values[pair_count:]
    energy_rows = lax.dynamic_slice_in_dim(vir_energy, aux_index * row_count, row_count, 1)
    denominator = energy_rows[:, :, None] + vir_energy[:, None, :] - occ_sum[:, None, None]
    updated = (
        amplitudes.astype(jnp.float32) - (cycle_term + k_term.astype(jnp.float32)) / denominator
    )
    return updated.astype(jnp.bfloat16)


def solution(mesh):
    placed = (
        P("pair", "aux", None),
        P("pair", "aux", None),
        P("pair", None, None),
        P("pair"),
        P("pair", "aux", None),
        P("pair", None),
        P(),
        P("pair", None),
    )
    return jax.shard_map(
        local, mesh=mesh, in_specs=placed, out_specs=P("pair", "aux", None), check_vma=False
    )
```

profile of v0, /device:TPU:2, one launch (start us, length us, event | category | flops | bytes accessed | tf_op | source)
XLA Modules:
  0.0 725.3 jit_solution(5603408930430910391)
XLA Ops:
  6.5 0.0 copy-start
  6.5 0.0 all-gather.2.cloned.1.call-start
  6.5 0.7 all-gather.2.cloned.1.call-update
  7.3 0.0 all-reduce.3.cloned.1.call-start
  7.3 0.7 fusion.24
  8.1 0.2 reduce_window_sum.11
  8.2 0.8 select_reduce_fusion.1
  9.1 0.7 fusion.28
  9.7 0.0 copy-done
  9.7 3.9 convolution_convert_fusion.1
  13.6 0.0 copy-start.3
  13.6 17.5 %all-gather.2.cloned.1.call-done = bf16[128,128,128]{2,1,0:T(8,128)(2,1)} async-done(((bf16[128,64,128]{2,1,0:T(8,128)(2,1)}), bf16[128,128,128]{2,1,0:T(8,128)(2,1)}) %all-gather.2.cloned.1.call-update) | async-done | bytes 4194320 | tf_op jit(solution)/shard_map/all_gather | solution.py:22
  31.1 9.4 %fusion.11 = bf16[128,128,128]{2,1,0:T(8,128)(2,1)} fusion(bf16[128,128,128]{2,1,0:T(8,128)(2,1)} %all-gather.2.cloned.1.call-done, bf16[128,128,128]{2,0,1:T(8,128)(2,1)} %convolution_convert_fusion.1), kind=kOutput, calls=%fused_computation.10 | convolution fusion | flops 536870912 | bytes 12582912 | tf_op jit(solution)/shard_map/pca,pab->pcb/dot_general | solution.py:29
  40.5 0.0 copy-done.3
  40.5 11.1 %convolution_convert_fusion = bf16[128,128,256]{2,1,0:T(8,128)(2,1)} fusion(bf16[128,128,128]{2,1,0:T(8,128)(2,1)} %fusion.11, bf16[128,128,128]{2,0,1:T(8,128)(2,1)} %convolution_convert_fusion.1, bf16[1,256,128]{2,1,0:T(8,128)(2,1)S(1)} %copy-done.3), kind=kOutput, calls=%fused_computation.4 | convolution fusion | flops 1616904192 | bytes 16842752 | tf_op jit(solution)/shard_map/pca,qa->pcq/dot_general | solution.py:35
  51.6 6.0 broadcast_in_dim.7
  57.5 23.5 %scatter_fusion = bf16[256,128,256]{2,1,0:T(8,128)(2,1)} fusion(bf16[256,128,256]{2,1,0:T(8,128)(2,1)} %broadcast_in_dim.7, s32[128]{0:T(128)S(1)} %fusion.28, bf16[128,128,256]{2,1,0:T(8,128)(2,1)} %convolution_convert_fusion), kind=kCustom, calls=%fused_computation.1 | custom fusion | bytes 25166336 | tf_op jit(solution)/shard_map/scatter | solution.py:47
  81.0 381.3 %all_to_all.10 = bf16[128,2,128,256]{3,2,1,0:T(8,128)(2,1)S(1)} all-to-all(bf16[128,2,128,256]{3,2,1,0:T(8,128)(2,1)} %bitcast.23), channel_id=1, replica_groups=mesh['pair'=128,'aux'=2] {'pair'}, dimensions={0} | all-to-all | bytes 33554432 | tf_op jit(solution)/shard_map/all_to_all | solution.py:50
  462.3 8.9 %fusion = bf16[1,128,256,1]{2,0,3,1:T(2,128)(2,1)S(1)} fusion(bf16[128,2,128,256]{3,2,1,0:T(8,128)(2,1)S(1)} %all_to_all.10), kind=kOutput, calls=%fused_computation.2 | convolution fusion | flops 16777216 | bytes 16842752 | tf_op jit(solution)/shard_map/sk,skcq->cq/dot_general | solution.py:52
  471.2 0.8 fusion.21
  472.0 0.0 all-reduce.3.cloned.1.call-update
  472.0 23.3 %all-reduce.3.cloned.1.call-done = f32[128,128]{1,0:T(8,128)} async-done(((f32[128,128]{1,0:T(8,128)}), f32[128,128]{1,0:T(8,128)}) %all-reduce.3.cloned.1.call-update) | async-done | bytes 65552 | tf_op jit(solution)/shard_map/psum | solution.py:56
  495.3 0.8 multiply_convert_fusion
  496.1 5.3 broadcast_in_dim.8
  501.5 0.0 copy-start.5
  501.5 0.0 copy-start.4
  501.5 0.0 copy-start.6
  501.5 14.5 %all-to-all-start.1 = ((bf16[128,2,128,128]{3,2,1,0:T(8,128)(2,1)}), bf16[128,2,128,128]{3,2,1,0:T(8,128)(2,1)}, u32[]{:S(2)}, u32[]{:S(2)}) async-start(bf16[128,2,128,128]{3,2,1,0:T(8,128)(2,1)} %broadcast_in_dim.8), calls=%async_computation.1 | async-start | bytes 16777216 | tf_op jit(solution)/shard_map/all_to_all | solution.py:62
  516.0 0.0 copy-done.5
  516.0 0.0 copy-done.4
  516.0 0.1 constant_dynamic-slice_fusion
  516.1 0.0 copy-done.6
  516.1 0.2 select_reduce_fusion
  516.3 187.0 %all-to-all-done.1 = bf16[128,2,128,128]{3,2,1,0:T(8,128)(2,1)} async-done(((bf16[128,2,128,128]{3,2,1,0:T(8,128)(2,1)}), bf16[128,2,128,128]{3,2,1,0:T(8,128)(2,1)}, u32[]{:S(2)}, u32[]{:S(2)}) %all-to-all-start.1) | async-done | bytes 8388640 | tf_op jit(solution)/shard_map/all_to_all | solution.py:62
  703.3 0.0 copy-start.2
  703.3 6.6 gather_fusion
  709.8 0.0 copy-done.2
  709.8 0.0 copy-start.1
  709.8 8.6 %subtract_convert_fusion = bf16[128,64,128]{2,1,0:T(8,128)(2,1)} fusion(bf16[128,64,128]{2,1,0:T(8,128)(2,1)} %param.9, bf16[128,64,128]{2,1,0:T(8,128)(2,1)S(1)} %copy-done.2, f32[128]{0:T(128)S(1)} %slice_add_fusion, f32[128,128]{1,0:T(8,128)S(1)} %copy-done.4, f32[128,64]{1,0:T(8,128)S(1)} %constant_dynamic-slice_fusion, ...), kind=kOutput, calls=%fused_computation.5 | convolution fusion | flops 276824064 | bytes 12681732 | tf_op jit(solution)/shard_map/pca,pba->pcb/dot_general | solution.py:65
  718.5 0.0 copy-done.1
  (3 shorter events, 0.0 us)
Async XLA Ops:
  6.5 3.2 copy-start
  6.5 24.6 %all-gather.2.cloned.1.call-start = ((), (), s32[]{:S(2)}) async-start(), calls=%async_computation.2 | async-start | bytes 6291456 | tf_op jit(solution)/shard_map/all_gather | solution.py:22
  7.3 488.0 %all-reduce.3.cloned.1.call-start = ((), (), s32[]{:S(2)}) async-start(), calls=%async_computation.3 | async-start | bytes 131072 | tf_op jit(solution)/shard_map/psum | solution.py:56
  13.6 26.9 %copy-start.3 = (bf16[1,256,128]{2,1,0:T(8,128)(2,1)S(1)}, bf16[1,256,128]{2,1,0:T(8,128)(2,1)}, u32[]{:S(2)}) copy-start(bf16[1,256,128]{2,1,0:T(8,128)(2,1)} %param.12) | copy-start | bytes 196612
  501.5 14.5 %copy-start.5 = (s32[128,1]{0,1:T(1,128)S(1)}, s32[128,1]{0,1:T(1,128)}, u32[]{:S(2)}) copy-start(s32[128,1]{0,1:T(1,128)} %param.15) | copy-start | bytes 1540
  501.5 14.5 %copy-start.4 = (f32[128,128]{1,0:T(8,128)S(1)}, f32[128,128]{1,0:T(8,128)}, u32[]{:S(2)}) copy-start(f32[128,128]{1,0:T(8,128)} %param.13) | copy-start | bytes 196612
  501.5 14.6 %copy-start.6 = (f32[128]{0:T(128)S(1)}, f32[128]{0:T(128)}, u32[]{:S(2)}) copy-start(f32[128]{0:T(128)} %param.14) | copy-start | bytes 1540
  501.5 201.8 %all-to-all-start.1 = ((bf16[128,2,128,128]{3,2,1,0:T(8,128)(2,1)}), bf16[128,2,128,128]{3,2,1,0:T(8,128)(2,1)}, u32[]{:S(2)}, u32[]{:S(2)}) async-start(bf16[128,2,128,128]{3,2,1,0:T(8,128)(2,1)} %broadcast_in_dim.8), calls=%async_computation.1 | async-start | bytes 16777216 | tf_op jit(solution)/shard_map/all_to_all | solution.py:62
  703.3 6.6 copy-start.2
  709.8 8.6 %copy-start.1 = (bf16[8,128,128]{2,1,0:T(8,128)(2,1)S(1)}, bf16[8,128,128]{2,1,0:T(8,128)(2,1)}, u32[]{:S(2)}) copy-start(bf16[8,128,128]{2,1,0:T(8,128)(2,1)} %param.10) | copy-start | bytes 786436
Sparse Core Ops, SparseCore 0:
  9.1 21.9 all-gather.1
  472.1 23.1 all-reduce.2
where the time goes:
time: 726 us; the launch traced here: 725 us
  blocking collectives  381 us (52%)
  waiting for transfers between devices  229 us (32%)
  matrix products  42.6 us (6%)
  local copies, waits for them, and re-layouts  41.4 us (6%)
  starting transfers between devices  14.5 us (2%)
  between operations  13.5 us (2%)
    all_to_all x1, blocking collectives, local(): lax.all_to_all(outgoing, 'pair', split_axis=0, concat_axis=0, tiled=True)  381 us
    all_to_all x1, waiting for transfers between devices, local(): lax.all_to_all(slot_back, 'pair', split_axis=0, concat_axis=0, tiled=True)  187 us
    scatter x1, local copies, waits for them, and re-layouts, local(): outgoing = jnp.zeros((axis_pairs * capacity, vir_width, aux_rows), jnp.bf...  23.5 us
    psum x1, waiting for transfers between devices, local(): cycle_sum = lax.psum(local_cycle, 'aux')  23.3 us
    all_gather x1, waiting for transfers between devices, local(): full_amp = lax.all_gather(amplitudes, 'aux', axis=1, tiled=True)  17.5 us
  transfers between devices with their start and end apart: 3, of which 3 were waited for; matrix products, arithmetic and copies ran while one was open for 1% of the time, Pallas kernels for 0%

commit v1 on v0

--- a/solution.py
+++ b/solution.py
@@ -53,7 +53,7 @@
         "sk,skcq->cq", slot_ones, incoming, preferred_element_type=jnp.float32
     ).astype(jnp.bfloat16)
     local_cycle = jnp.dot(summed, own_factors, preferred_element_type=jnp.float32)
-    cycle_sum = lax.psum(local_cycle, "aux")
+    cycle_sum = jnp.sum(lax.all_gather(local_cycle, "aux"), axis=0)
     cycle_vals = (cycle_scale * cycle_sum).astype(jnp.bfloat16)
     cycle_rows = cycle_vals.shape[0]
     slot_back = jnp.broadcast_to(

time: 726 us -> 697 us (0.960)
  waiting for transfers between devices: 229 us -> 205 us
    psum x1 -> x0, waiting for transfers between devices: 23.3 us -> none  [local(): cycle_sum = lax.psum(local_cycle, 'aux')]
  transfers between devices with their start and end apart: 3 -> 2, of which waited for: 3 -> 2; matrix products, arithmetic and copies ran while one was open for 1% -> 1% of each run, Pallas kernels for 0% -> 0%
where the time goes in v1:
time: 697 us; the launch traced here: 696 us
  blocking collectives  383 us (55%)
  waiting for transfers between devices  205 us (29%)
  matrix products  42 us (6%)
  local copies, waits for them, and re-layouts  41.3 us (6%)
  between operations  13.5 us (2%)
  starting transfers between devices  8.22 us (1%)
    all_to_all x1, blocking collectives, local(): lax.all_to_all(outgoing, 'pair', split_axis=0, concat_axis=0, tiled=True)  381 us
    all_to_all x1, waiting for transfers between devices, local(): lax.all_to_all(slot_back, 'pair', split_axis=0, concat_axis=0, tiled=True)  187 us
    scatter x1, local copies, waits for them, and re-layouts, local(): outgoing = jnp.zeros((axis_pairs * capacity, vir_width, aux_rows), jnp.bf...  23.3 us
    all_gather x1, waiting for transfers between devices, local(): full_amp = lax.all_gather(amplitudes, 'aux', axis=1, tiled=True)  17.5 us
  transfers between devices with their start and end apart: 2, of which 2 were waited for; matrix products, arithmetic and copies ran while one was open for 1% of the time, Pallas kernels for 0%

profile of v1, /device:TPU:2, one launch (start us, length us, event | category | flops | bytes accessed | tf_op | source)
XLA Modules:
  0.0 696.3 jit_solution(3616004471943296839)
XLA Ops:
  6.5 0.0 copy-start
  6.5 0.0 all-gather.3.cloned.1.call-start
  6.5 0.7 all-gather.3.cloned.1.call-update
  7.3 0.7 fusion.24
  8.0 0.2 reduce_window_sum.11
  8.2 0.8 select_reduce_fusion.1
  9.0 0.7 fusion.28
  9.7 0.0 copy-done
  9.7 3.9 convolution_convert_fusion.1
  13.6 0.0 copy-start.3
  13.6 17.5 %all-gather.3.cloned.1.call-done = bf16[128,128,128]{2,1,0:T(8,128)(2,1)} async-done(((bf16[128,64,128]{2,1,0:T(8,128)(2,1)}), bf16[128,128,128]{2,1,0:T(8,128)(2,1)}) %all-gather.3.cloned.1.call-update) | async-done | bytes 4194320 | tf_op jit(solution)/shard_map/all_gather | solution.py:22
  31.1 9.4 %fusion.11 = bf16[128,128,128]{2,1,0:T(8,128)(2,1)} fusion(bf16[128,128,128]{2,1,0:T(8,128)(2,1)} %all-gather.3.cloned.1.call-done, bf16[128,128,128]{2,0,1:T(8,128)(2,1)} %convolution_convert_fusion.1), kind=kOutput, calls=%fused_computation.10 | convolution fusion | flops 536870912 | bytes 12582912 | tf_op jit(solution)/shard_map/pca,pab->pcb/dot_general | solution.py:29
  40.5 0.0 copy-done.3
  40.5 11.1 %convolution_convert_fusion = bf16[128,128,256]{2,1,0:T(8,128)(2,1)} fusion(bf16[128,128,128]{2,1,0:T(8,128)(2,1)} %fusion.11, bf16[128,128,128]{2,0,1:T(8,128)(2,1)} %convolution_convert_fusion.1, bf16[1,256,128]{2,1,0:T(8,128)(2,1)S(1)} %copy-done.3), kind=kOutput, calls=%fused_computation.4 | convolution fusion | flops 1616904192 | bytes 16842752 | tf_op jit(solution)/shard_map/pca,qa->pcq/dot_general | solution.py:35
  51.6 6.0 broadcast_in_dim.7
  57.5 23.3 %scatter_fusion = bf16[256,128,256]{2,1,0:T(8,128)(2,1)} fusion(bf16[256,128,256]{2,1,0:T(8,128)(2,1)} %broadcast_in_dim.7, s32[128]{0:T(128)S(1)} %fusion.28, bf16[128,128,256]{2,1,0:T(8,128)(2,1)} %convolution_convert_fusion), kind=kCustom, calls=%fused_computation.1 | custom fusion | bytes 25166336 | tf_op jit(solution)/shard_map/scatter | solution.py:47
  80.9 381.4 %all_to_all.10 = bf16[128,2,128,256]{3,2,1,0:T(8,128)(2,1)S(1)} all-to-all(bf16[128,2,128,256]{3,2,1,0:T(8,128)(2,1)} %bitcast.24), channel_id=1, replica_groups=mesh['pair'=128,'aux'=2] {'pair'}, dimensions={0} | all-to-all | bytes 33554432 | tf_op jit(solution)/shard_map/all_to_all | solution.py:50
  462.3 8.9 %fusion = bf16[1,128,256,1]{2,0,3,1:T(2,128)(2,1)S(1)} fusion(bf16[128,2,128,256]{3,2,1,0:T(8,128)(2,1)S(1)} %all_to_all.10), kind=kOutput, calls=%fused_computation.2 | convolution fusion | flops 16777216 | bytes 16842752 | tf_op jit(solution)/shard_map/sk,skcq->cq/dot_general | solution.py:52
  471.2 0.1 fusion.21
  471.3 1.9 all-gather
  473.2 5.3 broadcast_in_dim.8
  478.6 0.0 copy-start.5
  478.6 0.0 copy-start.4
  478.6 0.0 copy-start.6
  478.6 8.2 %all-to-all-start.1 = ((bf16[128,2,128,128]{3,2,1,0:T(8,128)(2,1)}), bf16[128,2,128,128]{3,2,1,0:T(8,128)(2,1)}, u32[]{:S(2)}, u32[]{:S(2)}) async-start(bf16[128,2,128,128]{3,2,1,0:T(8,128)(2,1)} %broadcast_in_dim.8), calls=%async_computation.1 | async-start | bytes 16777216 | tf_op jit(solution)/shard_map/all_to_all | solution.py:62
  486.8 0.0 copy-done.5
  486.8 0.0 copy-done.4
  486.8 0.1 constant_dynamic-slice_fusion
  486.9 0.0 copy-done.6
  486.9 0.2 select_reduce_fusion
  487.1 187.1 %all-to-all-done.1 = bf16[128,2,128,128]{3,2,1,0:T(8,128)(2,1)} async-done(((bf16[128,2,128,128]{3,2,1,0:T(8,128)(2,1)}), bf16[128,2,128,128]{3,2,1,0:T(8,128)(2,1)}, u32[]{:S(2)}, u32[]{:S(2)}) %all-to-all-start.1) | async-done | bytes 8388640 | tf_op jit(solution)/shard_map/all_to_all | solution.py:62
  674.2 0.0 copy-start.2
  674.2 6.6 gather_fusion
  680.8 0.0 copy-done.2
  680.8 0.0 copy-start.1
  680.8 8.6 %subtract_convert_fusion = bf16[128,64,128]{2,1,0:T(8,128)(2,1)} fusion(bf16[128,64,128]{2,1,0:T(8,128)(2,1)} %param.9, bf16[128,64,128]{2,1,0:T(8,128)(2,1)S(1)} %copy-done.2, f32[128]{0:T(128)S(1)} %slice_add_fusion, f32[128,128]{1,0:T(8,128)S(1)} %copy-done.4, f32[128,64]{1,0:T(8,128)S(1)} %constant_dynamic-slice_fusion, ...), kind=kOutput, calls=%fused_computation.5 | convolution fusion | flops 276824064 | bytes 12681732 | tf_op jit(solution)/shard_map/pca,pba->pcb/dot_general | solution.py:65
  689.4 0.0 copy-done.1
  (5 shorter events, 0.0 us)
Async XLA Ops:
  6.5 3.1 copy-start
  6.5 24.6 %all-gather.3.cloned.1.call-start = ((), (), s32[]{:S(2)}) async-start(), calls=%async_computation.2 | async-start | bytes 6291456 | tf_op jit(solution)/shard_map/all_gather | solution.py:22
  13.6 26.9 %copy-start.3 = (bf16[1,256,128]{2,1,0:T(8,128)(2,1)S(1)}, bf16[1,256,128]{2,1,0:T(8,128)(2,1)}, u32[]{:S(2)}) copy-start(bf16[1,256,128]{2,1,0:T(8,128)(2,1)} %param.12) | copy-start | bytes 196612
  478.6 8.2 %copy-start.5 = (s32[128,1]{0,1:T(1,128)S(1)}, s32[128,1]{0,1:T(1,128)}, u32[]{:S(2)}) copy-start(s32[128,1]{0,1:T(1,128)} %param.15) | copy-start | bytes 1540
  478.6 8.3 %copy-start.4 = (f32[128,128]{1,0:T(8,128)S(1)}, f32[128,128]{1,0:T(8,128)}, u32[]{:S(2)}) copy-start(f32[128,128]{1,0:T(8,128)} %param.13) | copy-start | bytes 196612
  478.6 8.4 %copy-start.6 = (f32[128]{0:T(128)S(1)}, f32[128]{0:T(128)}, u32[]{:S(2)}) copy-start(f32[128]{0:T(128)} %param.14) | copy-start | bytes 1540
  478.6 195.6 %all-to-all-start.1 = ((bf16[128,2,128,128]{3,2,1,0:T(8,128)(2,1)}), bf16[128,2,128,128]{3,2,1,0:T(8,128)(2,1)}, u32[]{:S(2)}, u32[]{:S(2)}) async-start(bf16[128,2,128,128]{3,2,1,0:T(8,128)(2,1)} %broadcast_in_dim.8), calls=%async_computation.1 | async-start | bytes 16777216 | tf_op jit(solution)/shard_map/all_to_all | solution.py:62
  674.2 6.6 copy-start.2
  680.8 8.6 %copy-start.1 = (bf16[8,128,128]{2,1,0:T(8,128)(2,1)S(1)}, bf16[8,128,128]{2,1,0:T(8,128)(2,1)}, u32[]{:S(2)}) copy-start(bf16[8,128,128]{2,1,0:T(8,128)(2,1)} %param.10) | copy-start | bytes 786436
Sparse Core Ops, SparseCore 0:
  9.1 21.9 all-gather.2
